TPU v7x, 256 devices: a whole 4x4x8 slice. The times are simulated.
256 devices in a mesh: row: 8 (over x, core), pair: 32 (over y, z).
Axes of the slice: x: 4, y: 4, z: 8, core: 2. Of those that a mesh axis runs over, the one named last changes fastest.
Arguments:
- weight: float32 [28672, 8192], P('row', 'pair'), may hold values from -300 to 300
- move_flags: int32 [2, 32], P(None, 'pair'), may hold values from 0 to 1
Outputs:
- columns: float32 [28672, 8192], P('row', 'pair')
- norm_ratios: float32 [8192], P('pair')
All inputs are finite; a program needn't handle non-finite values.
Results may differ from a plain program's by a relative error of at most 0.0003.
Values sent between devices are 32-bit elements; how exact they have to be, the bound alone decides.
No kernel may reach another device: no remote copies, remote signals or barrier semaphores. Data moves between devices by JAX's collectives and lax.ppermute only.
A program may use at most 64 MiB of HBM per device.

v0:
```python
import jax
import jax.numpy as jnp
from jax import lax
from jax.sharding import PartitionSpec as P

SWEEPS = 2
POLAR = 8
ROUNDS = 3


precise = lax.Precision.HIGHEST


def from_behind(block, axis, distance):
    devices = range(lax.axis_size(axis))
    route = [((i - distance) % len(devices), i) for i in devices]
    return lax.ppermute(block, axis, route)


def contract(left, right):
    return lax.dot_general(
        left, right, (((0,), (0,)), ((), ())), precision=precise, preferred_element_type=jnp.float32
    )


def orthogonal_iteration(gram_pair):
    rotation = jnp.eye(gram_pair.shape[0], dtype=jnp.float32)
    for sweep_index in range(SWEEPS):
        product = jnp.dot(
            gram_pair, rotation, precision=precise, preferred_element_type=jnp.float32
        )
        normal = contract(product, product)
        scaled = product / jnp.sqrt(jnp.sqrt(jnp.sum(normal * normal)))
        for polar_index in range(POLAR):
            inner = contract(scaled, scaled)
            scaled = 1.5 * scaled - 0.5 * jnp.dot(
                scaled, inner, precision=precise, preferred_element_type=jnp.float32
            )
        rotation = scaled
    return rotation


def on_device(weight, move_flags):
    half_width = weight.shape[1] // 2
    row_count = weight.shape[0] * lax.axis_size("row")
    cell_count = row_count * weight.shape[1] * lax.axis_size("pair")
    current = weight
    rotated = weight
    turned = None
    for round_index in range(ROUNDS):
        gram_pair = lax.psum(contract(current, current), "row")
        rotation = orthogonal_iteration(gram_pair)
        if round_index + 1 < ROUNDS:
            swapped = jnp.concatenate([rotation[:, half_width:], rotation[:, :half_width]], axis=1)
            rotation = jnp.where(move_flags[round_index, 0] == 1, swapped, rotation)
        rotated = jnp.dot(current, rotation, precision=precise, preferred_element_type=jnp.float32)
        turned = contract(
            rotation,
            jnp.dot(gram_pair, rotation, precision=precise, preferred_element_type=jnp.float32),
        )
        if round_index + 1 < ROUNDS:
            staying = rotated[:, :half_width]
            arrived = from_behind(rotated[:, half_width:], "pair", 1)
            current = jnp.concatenate([staying, arrived], axis=1)
    squares_total = lax.psum(jnp.trace(turned), "pair")
    divisor = jnp.sqrt(squares_total / cell_count)
    columns = rotated / divisor
    norm_ratios = jnp.sqrt(jnp.diagonal(turned) / row_count) / divisor
    return (columns, norm_ratios)


def solution(mesh):
    return jax.shard_map(
        on_device,
        mesh=mesh,
        in_specs=(P("row", "pair"), P(None, "pair")),
        out_specs=(P("row", "pair"), P("pair")),
        check_vma=False,
    )
```

profile of v0, /device:TPU:4, one launch (start us, length us, event | category | flops | bytes accessed | tf_op | source)
XLA Modules:
  0.0 481.2 jit_solution(14597341198546668713)
XLA Ops:
  7.2 9.8 %fusion.82 = f32[256,256]{1,0:T(8,128)} fusion(f32[3584,256]{1,0:T(8,128)} %param.2), kind=kOutput, calls=%fused_computation.153 | convolution fusion | flops 2818572288 | bytes 3932160 | tf_op jit(solution)/shard_map/dot_general | solution.py:21
  17.6 0.7 fusion.81
  18.9 62.7 %all-reduce.4.cloned.1.call-done = f32[256,256]{1,0:T(8,128)} async-done(((f32[256,256]{1,0:T(8,128)}), f32[256,256]{1,0:T(8,128)}) %all-reduce.4.cloned.1.call-update) | async-done | bytes 262160 | tf_op jit(solution)/shard_map/psum | solution.py:51
  81.7 1.2 fusion.63
  82.9 1.2 fusion.51
  84.8 0.6 fusion.66
  85.8 0.6 fusion.83
  86.8 0.6 fusion.84
  87.8 0.6 fusion.85
  88.8 0.6 fusion.86
  89.8 0.6 fusion.87
  90.8 0.6 fusion.88
  91.8 0.6 fusion.89
  93.5 1.0 fusion.52
  95.3 0.6 fusion.67
  96.3 0.6 fusion.91
  97.3 0.6 fusion.92
  98.4 0.6 fusion.93
  100.4 0.6 fusion.95
  101.4 0.6 fusion.96
  103.5 6.2 %convolution_bitcast_fusion = f32[3584,256]{0,1:T(8,128)S(1)} fusion(f32[3584,256]{1,0:T(8,128)S(1)} %copy-done, f32[256,256]{1,0:T(8,128)S(1)} %fusion.35, f32[256,128]{1,0:T(8,128)S(1)} %get-tuple-element.9, f32[256,128]{1,0:T(8,128)S(1)} %get-tuple-element.8, pred[]{:T(512)} %bitcast), kind=kOutput, calls=%fused_computation.1 | convolution fusion | flops 2818703360 | bytes 7864321 | tf_op jit(solution)/shard_map/dot_general | solution.py:56
  109.9 1.6 collective-permute-start
  111.5 44.6 %collective-permute-done = f32[3584,128]{0,1:T(8,128)S(1)} collective-permute-done((f32[3584,128]{0,1:T(8,128)S(1)}, f32[3584,128]{0,1:T(8,128)S(1)}, u32[]{:S(2)}, u32[]{:S(2)}) %collective-permute-start) | collective-permute-done | bytes 1835040 | tf_op jit(solution)/shard_map/ppermute | solution.py:17
  156.1 1.2 copy-done.2
  157.4 3.8 fusion.2
  162.3 60.7 %all-reduce.6.cloned.1.call-done = f32[256,256]{1,0:T(8,128)} async-done(((f32[256,256]{1,0:T(8,128)}), f32[256,256]{1,0:T(8,128)}) %all-reduce.6.cloned.1.call-update) | async-done | bytes 262160 | tf_op jit(solution)/shard_map/psum | solution.py:51
  223.1 1.2 fusion.62
  224.3 1.2 fusion.53
  226.2 0.6 fusion.68
  227.2 0.6 fusion.98
  228.2 0.6 fusion.99
  229.2 0.6 fusion.100
  233.2 0.6 fusion.104
  235.0 1.0 fusion.54
  236.7 0.6 fusion.69
  237.7 0.6 fusion.106
  238.7 0.6 fusion.107
  241.9 0.6 fusion.110
  242.8 0.6 fusion.111
  244.9 3.7 fusion.1
  248.8 1.8 collective-permute-start.1
  250.7 44.6 %collective-permute-done.1 = f32[3584,128]{0,1:T(8,128)S(1)} collective-permute-done((f32[3584,128]{0,1:T(8,128)S(1)}, f32[3584,128]{0,1:T(8,128)S(1)}, u32[]{:S(2)}, u32[]{:S(2)}) %collective-permute-start.1) | collective-permute-done | bytes 1835040 | tf_op jit(solution)/shard_map/ppermute | solution.py:17
  295.3 1.3 copy-done.7
  296.5 3.8 fusion
  300.4 62.0 %all-reduce.8.cloned.1.call-done = f32[256,256]{1,0:T(8,128)} async-done(((f32[256,256]{1,0:T(8,128)}), f32[256,256]{1,0:T(8,128)}) %all-reduce.8.cloned.1.call-update) | async-done | bytes 262160 | tf_op jit(solution)/shard_map/psum | solution.py:51
  362.3 1.2 fusion.61
  363.6 1.2 fusion.55
  365.5 0.6 fusion.70
  367.5 0.6 fusion.114
  370.5 0.6 fusion.117
  371.5 0.6 fusion.118
  372.5 0.6 fusion.119
  373.5 0.8 fusion.120
  374.3 1.2 fusion.56
  376.2 0.6 fusion.71
  377.2 0.6 fusion.121
  378.2 0.6 fusion.122
  379.2 0.6 fusion.123
  382.2 0.6 fusion.126
  383.2 0.6 fusion.127
  384.5 1.2 select_reduce_fusion
  385.7 75.9 %psum.31 = f32[]{:T(128)} all-reduce(f32[]{:T(128)} %get-tuple-element.12), channel_id=1, replica_groups=mesh['row'=8,'pair'=32] {'pair'}, use_global_device_ids=true, to_apply=%region_10.11 | all-reduce | flops 1 | bytes 8 | tf_op jit(solution)/shard_map/psum | solution.py:65
  462.3 2.3 gather_fusion
  465.3 9.2 %convolution_divide_fusion = f32[3584,256]{1,0:T(8,128)} fusion(f32[256,256]{1,0:T(8,128)S(1)} %fusion.3, f32[3584,128]{0,1:T(8,128)} %copy-done.7, f32[3584,128]{0,1:T(8,128)S(1)} %get-tuple-element.2, f32[]{:T(128)S(6)} %sqrt.54), kind=kOutput, calls=%fused_computation.2 | convolution fusion | flops 2820407296 | bytes 7602180 | tf_op jit(solution)/shard_map/dot_general | solution.py:56
  (92 shorter events, 30.5 us)
Async XLA Ops:
  7.2 10.4 %copy-start.6 = (s32[2,1]{0,1:T(1,128)S(1)}, s32[2,1]{0,1:T(1,128)}, u32[]{:S(2)}) copy-start(s32[2,1]{0,1:T(1,128)} %param.3) | copy-start | bytes 28
  7.2 74.5 %all-reduce.4.cloned.1.call-start = ((), (), s32[]{:S(2)}) async-start(), calls=%async_computation | async-start | bytes 524288 | tf_op jit(solution)/shard_map/psum | solution.py:51
  17.0 206.0 %all-reduce.6.cloned.1.call-start = ((), (), s32[]{:S(2)}) async-start(), calls=%async_computation.1 | async-start | bytes 524288 | tf_op jit(solution)/shard_map/psum | solution.py:51
  88.4 4.4 copy-start.4
  99.0 4.4 copy-start
  109.9 46.2 %collective-permute-start = (f32[3584,128]{0,1:T(8,128)S(1)}, f32[3584,128]{0,1:T(8,128)S(1)}, u32[]{:S(2)}, u32[]{:S(2)}) collective-permute-start(f32[3584,128]{0,1:T(8,128)S(1)} %get-tuple-element.5), channel_id=1, source_target_pairs={{31,0},{0,1},{1,2},{2,3},{3,4},{4,5},{5,6},{6,7},{7,8},{8,9},{9,10... | collective-permute-start | bytes 5505032 | tf_op jit(solution)/shard_map/ppermute | solution.py:17
  156.1 1.2 copy-start.2
  161.2 201.1 %all-reduce.8.cloned.1.call-start = ((), (), s32[]{:S(2)}) async-start(), calls=%async_computation.2 | async-start | bytes 524288 | tf_op jit(solution)/shard_map/psum | solution.py:51
  229.8 4.4 copy-start.5
  240.5 4.4 copy-start.3
  248.8 46.4 %collective-permute-start.1 = (f32[3584,128]{0,1:T(8,128)S(1)}, f32[3584,128]{0,1:T(8,128)S(1)}, u32[]{:S(2)}, u32[]{:S(2)}) collective-permute-start(f32[3584,128]{0,1:T(8,128)S(1)} %get-tuple-element.3), channel_id=1, source_target_pairs={{31,0},{0,1},{1,2},{2,3},{3,4},{4,5},{5,6},{6,7},{7,8},{8,9},{9,10... | collective-permute-start | bytes 5505032 | tf_op jit(solution)/shard_map/ppermute | solution.py:17
  295.3 1.3 copy-start.7
  369.1 4.4 copy-start.1
Sparse Core Ops, SparseCore 0:
  17.2 64.4 all-reduce.3
  161.3 61.7 all-reduce.5
  300.5 61.8 all-reduce.7
where the time goes:
time: 488 us; the launch traced here: 481 us
  waiting for transfers between devices  275 us (56%)
  matrix products  97.9 us (20%)
  blocking collectives  75.9 us (16%)
  between operations  21.4 us (4%)
  local copies, waits for them, and re-layouts  6.3 us (1%)
    psum x3, waiting for transfers between devices, on_device(): gram_pair = lax.psum(contract(current, current), 'row')  185 us
    ppermute x2, waiting for transfers between devices, from_behind(): return lax.ppermute(block, axis, route)  89.2 us
    psum x1, blocking collectives, on_device(): squares_total = lax.psum(jnp.trace(turned), 'pair')  75.9 us
    dot_general x58, matrix products, contract(): lax.dot_general(left, right, (((0,), (0,)), ((), ())), precision=precise,...  54.1 us
    dot_general x3, matrix products, on_device(): jnp.dot(current, rotation, precision=precise, preferred_element_type=jnp....  19.1 us
    dot_general x48, matrix products, orthogonal_iteration(): jnp.dot(scaled, inner, precision=precise, preferred_element_type=jnp.floa...  18.7 us
  transfers between devices with their start and end apart: 5, of which 5 were waited for; matrix products, arithmetic and copies ran while one was open for 0% of the time, Pallas kernels for 0%

commit v1 on v0

--- a/solution.py
+++ b/solution.py
@@ -15,6 +15,18 @@
     devices = range(lax.axis_size(axis))
     route = [((i - distance) % len(devices), i) for i in devices]
     return lax.ppermute(block, axis, route)
+
+
+def butterfly_sum(value, axis):
+    size = lax.axis_size(axis)
+    if size & (size - 1):
+        return lax.psum(value, axis)
+    step = 1
+    while step < size:
+        route = [(i, i ^ step) for i in range(size)]
+        value = value + lax.ppermute(value, axis, route)
+        step *= 2
+    return value
 
 
 def contract(left, right):
@@ -48,24 +60,26 @@
     rotated = weight
     turned = None
     for round_index in range(ROUNDS):
-        gram_pair = lax.psum(contract(current, current), "row")
+        gram_pair = butterfly_sum(contract(current, current), "row")
         rotation = orthogonal_iteration(gram_pair)
         if round_index + 1 < ROUNDS:
             swapped = jnp.concatenate([rotation[:, half_width:], rotation[:, :half_width]], axis=1)
             rotation = jnp.where(move_flags[round_index, 0] == 1, swapped, rotation)
         rotated = jnp.dot(current, rotation, precision=precise, preferred_element_type=jnp.float32)
-        turned = contract(
-            rotation,
-            jnp.dot(gram_pair, rotation, precision=precise, preferred_element_type=jnp.float32),
-        )
         if round_index + 1 < ROUNDS:
             staying = rotated[:, :half_width]
             arrived = from_behind(rotated[:, half_width:], "pair", 1)
             current = jnp.concatenate([staying, arrived], axis=1)
-    squares_total = lax.psum(jnp.trace(turned), "pair")
+        else:
+            turned = jnp.sum(
+                rotation
+                * jnp.dot(gram_pair, rotation, precision=precise, preferred_element_type=jnp.float32),
+                axis=0,
+            )
+    squares_total = butterfly_sum(jnp.sum(turned), "pair")
     divisor = jnp.sqrt(squares_total / cell_count)
     columns = rotated / divisor
-    norm_ratios = jnp.sqrt(jnp.diagonal(turned) / row_count) / divisor
+    norm_ratios = jnp.sqrt(turned / row_count) / divisor
     return (columns, norm_ratios)
 
 

time: 488 us -> 296 us (0.61)
  waiting for transfers between devices: 275 us -> 155 us
  blocking collectives: 75.9 us -> 0 us
  starting transfers between devices: 4.52 us -> 16.4 us
  between operations: 21.4 us -> 11.6 us
  matrix products: 97.9 us -> 104 us
  local copies, waits for them, and re-layouts: 6.3 us -> 1.41 us
    psum x3 -> x0, waiting for transfers between devices: 185 us -> none  [on_device(): gram_pair = lax.psum(contract(current, current), 'row')]
    psum x1 -> x0, blocking collectives: 75.9 us -> none  [on_device(): squares_total = lax.psum(jnp.trace(turned), 'pair')]
    ppermute x0 -> x14, waiting for transfers between devices: none -> 66.7 us  [butterfly_sum(): value = value + lax.ppermute(value, axis, route)]
    ppermute x0 -> x14, starting transfers between devices: none -> 14.3 us  [butterfly_sum(): value = value + lax.ppermute(value, axis, route)]
    dot_general x58 -> x57, matrix products: 54.1 us -> 62.8 us  [contract(): lax.dot_general(left, right, (((0,), (0,)), ((), ())), precision=precise,...]
  transfers between devices with their start and end apart: 5 -> 16, of which waited for: 5 -> 16; matrix products, arithmetic and copies ran while one was open for 0% -> 0% of each run, Pallas kernels for 0% -> 0%
where the time goes in v1:
time: 296 us; the launch traced here: 290 us
  waiting for transfers between devices  155 us (52%)
  matrix products  104 us (35%)
  starting transfers between devices  16.4 us (6%)
  between operations  11.6 us (4%)
    ppermute x2, waiting for transfers between devices, from_behind(): return lax.ppermute(block, axis, route)  88.6 us
    ppermute x14, waiting for transfers between devices, butterfly_sum(): value = value + lax.ppermute(value, axis, route)  66.7 us
    dot_general x57, matrix products, contract(): lax.dot_general(left, right, (((0,), (0,)), ((), ())), precision=precise,...  62.8 us
    dot_general x3, matrix products, on_device(): jnp.dot(current, rotation, precision=precise, preferred_element_type=jnp....  19.1 us
    dot_general x48, matrix products, orthogonal_iteration(): jnp.dot(scaled, inner, precision=precise, preferred_element_type=jnp.floa...  18.9 us
    ppermute x14, starting transfers between devices, butterfly_sum(): value = value + lax.ppermute(value, axis, route)  14.3 us
  transfers between devices with their start and end apart: 16, of which 16 were waited for; matrix products, arithmetic and copies ran while one was open for 0% of the time, Pallas kernels for 0%

profile of v1, /device:TPU:4, one launch (start us, length us, event | category | flops | bytes accessed | tf_op | source)
XLA Modules:
  0.0 289.9 jit_solution(10947977174320695368)
XLA Ops:
  0.6 9.1 %fusion.77 = f32[256,256]{1,0:T(8,128)S(1)} fusion(f32[3584,256]{1,0:T(8,128)} %param.2), kind=kOutput, calls=%fused_computation.152 | convolution fusion | flops 2818572288 | bytes 3932160 | tf_op jit(solution)/shard_map/dot_general | solution.py:33
  9.8 1.5 collective-permute-done
  11.4 1.3 collective-permute-start.1
  12.7 7.2 %collective-permute-done.1 = f32[256,256]{1,0:T(8,128)S(1)} collective-permute-done((f32[256,256]{1,0:T(8,128)S(1)}, f32[256,256]{1,0:T(8,128)S(1)}, u32[]{:S(2)}, u32[]{:S(2)}) %collective-permute-start.1) | collective-permute-done | bytes 262176 | tf_op jit(solution)/shard_map/ppermute | solution.py:27
  19.9 2.7 collective-permute-start.2
  22.5 0.6 fusion.76
  23.8 5.5 %collective-permute-done.2 = f32[256,256]{1,0:T(8,128)S(1)} collective-permute-done((f32[256,256]{1,0:T(8,128)S(1)}, f32[256,256]{1,0:T(8,128)S(1)}, u32[]{:S(2)}, u32[]{:S(2)}) %collective-permute-start.2) | collective-permute-done | bytes 262176 | tf_op jit(solution)/shard_map/ppermute | solution.py:27
  29.6 1.2 fusion.45
  31.6 0.6 fusion.60
  33.6 0.6 fusion.79
  34.6 0.6 fusion.80
  38.5 0.6 fusion.84
  39.5 0.6 fusion.85
  40.1 1.0 fusion.46
  42.0 0.6 fusion.61
  43.0 0.6 fusion.86
  44.0 12.7 %fusion.87 = f32[256,256]{1,0:T(8,128)S(1)} fusion(f32[256,256]{1,0:T(8,128)S(1)} %fusion.37), kind=kOutput, calls=%fused_computation.162 | convolution fusion | flops 201326592 | bytes 524288 | tf_op jit(solution)/shard_map/dot_general | solution.py:33
  59.1 0.6 fusion.90
  62.1 6.2 %convolution_bitcast_fusion = f32[3584,256]{0,1:T(8,128)S(1)} fusion(f32[3584,256]{1,0:T(8,128)S(1)} %copy-done, f32[256,256]{1,0:T(8,128)S(1)} %fusion.31, f32[256,128]{1,0:T(8,128)S(1)} %get-tuple-element.11, f32[256,128]{1,0:T(8,128)S(1)} %get-tuple-element.10, pred[]{:T(512)} %bitcast), kind=kOutput, calls=%fused_computation | convolution fusion | flops 2818703360 | bytes 7864321 | tf_op jit(solution)/shard_map/dot_general | solution.py:68
  68.5 2.0 collective-permute-start.3
  70.5 45.0 %collective-permute-done.3 = f32[3584,128]{0,1:T(8,128)S(1)} collective-permute-done((f32[3584,128]{0,1:T(8,128)S(1)}, f32[3584,128]{0,1:T(8,128)S(1)}, u32[]{:S(2)}, u32[]{:S(2)}) %collective-permute-start.3) | collective-permute-done | bytes 1835040 | tf_op jit(solution)/shard_map/ppermute | solution.py:17
  115.5 3.1 %fusion.2 = f32[256,256]{1,0:T(8,128)S(1)} fusion(f32[3584,128]{0,1:T(8,128)S(1)} %collective-permute-done.3, f32[3584,128]{0,1:T(8,128)S(1)} %get-tuple-element.6), kind=kOutput, calls=%fused_computation.6 | convolution fusion | flops 2819489792 | bytes 3932160 | tf_op jit(solution)/shard_map/dot_general | solution.py:33
  118.7 1.5 collective-permute-done.4
  120.3 1.3 collective-permute-start.5
  121.6 7.2 %collective-permute-done.5 = f32[256,256]{1,0:T(8,128)S(1)} collective-permute-done((f32[256,256]{1,0:T(8,128)S(1)}, f32[256,256]{1,0:T(8,128)S(1)}, u32[]{:S(2)}, u32[]{:S(2)}) %collective-permute-start.5) | collective-permute-done | bytes 262176 | tf_op jit(solution)/shard_map/ppermute | solution.py:27
  128.8 1.0 collective-permute-start.6
  130.4 7.9 %collective-permute-done.6 = f32[256,256]{1,0:T(8,128)S(1)} collective-permute-done((f32[256,256]{1,0:T(8,128)S(1)}, f32[256,256]{1,0:T(8,128)S(1)}, u32[]{:S(2)}, u32[]{:S(2)}) %collective-permute-start.6) | collective-permute-done | bytes 262176 | tf_op jit(solution)/shard_map/ppermute | solution.py:27
  138.6 1.2 fusion.47
  140.5 0.6 fusion.62
  143.5 0.6 fusion.95
  144.5 0.6 fusion.96
  147.5 0.6 fusion.99
  148.5 0.6 fusion.100
  149.1 1.0 fusion.48
  151.0 0.6 fusion.63
  152.0 0.6 fusion.101
  153.0 0.6 fusion.102
  156.1 0.6 fusion.105
  157.1 0.6 fusion.106
  158.1 0.6 fusion.107
  159.1 3.7 %fusion.1 = f32[3584,256]{0,1:T(8,128)S(1)} fusion(f32[3584,128]{0,1:T(8,128)S(1)} %copy-done.2, f32[3584,128]{0,1:T(8,128)S(1)} %get-tuple-element.6, f32[256,256]{1,0:T(8,128)S(1)} %fusion.17, f32[256,128]{1,0:T(8,128)S(1)} %get-tuple-element.9, f32[256,128]{1,0:T(8,128)S(1)} %get-tuple-element.8, pred[]{:T(512)} %bitcast.2), kind=kOutput, calls=%fused_computation.5 | convolution fusion | flops 2819620864 | bytes 7864321 | tf_op jit(solution)/shard_map/dot_general | solution.py:68
  163.2 43.6 %collective-permute-done.7 = f32[3584,128]{0,1:T(8,128)S(1)} collective-permute-done((f32[3584,128]{0,1:T(8,128)S(1)}, f32[3584,128]{0,1:T(8,128)S(1)}, u32[]{:S(2)}, u32[]{:S(2)}) %collective-permute-start.7) | collective-permute-done | bytes 1835040 | tf_op jit(solution)/shard_map/ppermute | solution.py:17
  206.8 3.1 %fusion = f32[256,256]{1,0:T(8,128)S(1)} fusion(f32[3584,128]{0,1:T(8,128)S(1)} %collective-permute-done.7, f32[3584,128]{0,1:T(8,128)S(1)} %get-tuple-element.4), kind=kOutput, calls=%fused_computation.4 | convolution fusion | flops 2819489792 | bytes 3932160 | tf_op jit(solution)/shard_map/dot_general | solution.py:33
  210.1 1.5 collective-permute-done.8
  211.6 1.3 collective-permute-start.9
  212.9 7.2 %collective-permute-done.9 = f32[256,256]{1,0:T(8,128)S(1)} collective-permute-done((f32[256,256]{1,0:T(8,128)S(1)}, f32[256,256]{1,0:T(8,128)S(1)}, u32[]{:S(2)}, u32[]{:S(2)}) %collective-permute-start.9) | collective-permute-done | bytes 262176 | tf_op jit(solution)/shard_map/ppermute | solution.py:27
  220.1 0.8 collective-permute-start.10
  220.9 8.5 %collective-permute-done.10 = f32[256,256]{1,0:T(8,128)S(1)} collective-permute-done((f32[256,256]{1,0:T(8,128)S(1)}, f32[256,256]{1,0:T(8,128)S(1)}, u32[]{:S(2)}, u32[]{:S(2)}) %collective-permute-start.10) | collective-permute-done | bytes 262176 | tf_op jit(solution)/shard_map/ppermute | solution.py:27
  229.7 1.2 fusion.49
  231.6 0.6 fusion.64
  240.0 1.2 fusion.50
  241.9 0.6 fusion.65
  244.5 0.8 fusion.8
  250.3 1.0 fusion.71
  251.3 3.7 %collective-permute-done.11 = f32[]{:T(128)} collective-permute-done((f32[]{:T(128)}, f32[]{:T(128)}, u32[]{:S(2)}, u32[]{:S(2)}) %collective-permute-start.11) | collective-permute-done | bytes 36 | tf_op jit(solution)/shard_map/ppermute | solution.py:27
  256.3 1.4 collective-permute-start.12
  257.7 3.1 %collective-permute-done.12 = f32[]{:T(128)} collective-permute-done((f32[]{:T(128)}, f32[]{:T(128)}, u32[]{:S(2)}, u32[]{:S(2)}) %collective-permute-start.12) | collective-permute-done | bytes 36 | tf_op jit(solution)/shard_map/ppermute | solution.py:27
  261.5 1.4 collective-permute-start.13
  262.9 6.1 %collective-permute-done.13 = f32[]{:T(128)} collective-permute-done((f32[]{:T(128)}, f32[]{:T(128)}, u32[]{:S(2)}, u32[]{:S(2)}) %collective-permute-start.13) | collective-permute-done | bytes 36 | tf_op jit(solution)/shard_map/ppermute | solution.py:27
  269.7 1.4 collective-permute-start.14
  271.1 2.2 collective-permute-done.14
  274.0 1.6 collective-permute-start.15
  275.5 3.7 %collective-permute-done.15 = f32[]{:T(128)} collective-permute-done((f32[]{:T(128)}, f32[]{:T(128)}, u32[]{:S(2)}, u32[]{:S(2)}) %collective-permute-start.15) | collective-permute-done | bytes 36 | tf_op jit(solution)/shard_map/ppermute | solution.py:27
  280.5 9.2 %convolution_divide_fusion = f32[3584,256]{1,0:T(8,128)} fusion(f32[256,256]{1,0:T(8,128)S(1)} %fusion.3, f32[3584,128]{0,1:T(8,128)} %copy-done.4, f32[3584,128]{0,1:T(8,128)S(1)} %get-tuple-element.4, f32[]{:T(128)S(6)} %sqrt.54), kind=kOutput, calls=%fused_computation.1 | convolution fusion | flops 2820407296 | bytes 7602180 | tf_op jit(solution)/shard_map/dot_general | solution.py:68
  (110 shorter events, 38.1 us)
Async XLA Ops:
  0.6 21.9 %copy-start.3 = (s32[2,1]{0,1:T(1,128)S(1)}, s32[2,1]{0,1:T(1,128)}, u32[]{:S(2)}) copy-start(s32[2,1]{0,1:T(1,128)} %param.3) | copy-start | bytes 28
  9.7 1.6 collective-permute-start
  11.4 8.4 %collective-permute-start.1 = (f32[256,256]{1,0:T(8,128)S(1)}, f32[256,256]{1,0:T(8,128)S(1)}, u32[]{:S(2)}, u32[]{:S(2)}) collective-permute-start(f32[256,256]{1,0:T(8,128)S(1)} %add.42), channel_id=1, source_target_pairs={{0,64},{32,96},{64,0},{96,32},{128,192},{160,224},{192,128},{224,1... | collective-permute-start | bytes 786440 | tf_op jit(solution)/shard_map/ppermute | solution.py:27
  19.9 9.5 %collective-permute-start.2 = (f32[256,256]{1,0:T(8,128)S(1)}, f32[256,256]{1,0:T(8,128)S(1)}, u32[]{:S(2)}, u32[]{:S(2)}) collective-permute-start(f32[256,256]{1,0:T(8,128)S(1)} %add.43), channel_id=1, source_target_pairs={{0,128},{32,160},{64,192},{96,224},{128,0},{160,32},{192,64},{224,... | collective-permute-start | bytes 786440 | tf_op jit(solution)/shard_map/ppermute | solution.py:27
  57.7 4.4 %copy-start = (f32[3584,256]{1,0:T(8,128)S(1)}, f32[3584,256]{1,0:T(8,128)}, u32[]{:S(2)}) copy-start(f32[3584,256]{1,0:T(8,128)} %param.2) | copy-start | bytes 11010052
  68.5 47.0 %collective-permute-start.3 = (f32[3584,128]{0,1:T(8,128)S(1)}, f32[3584,128]{0,1:T(8,128)S(1)}, u32[]{:S(2)}, u32[]{:S(2)}) collective-permute-start(f32[3584,128]{0,1:T(8,128)S(1)} %get-tuple-element.7), channel_id=1, source_target_pairs={{31,0},{0,1},{1,2},{2,3},{3,4},{4,5},{5,6},{6,7},{7,8},{8,9},{9,10... | collective-permute-start | bytes 5505032 | tf_op jit(solution)/shard_map/ppermute | solution.py:17
  115.5 22.7 %copy-start.1 = (f32[3584,128]{0,1:T(8,128)}, f32[3584,128]{0,1:T(8,128)S(1)}, u32[]{:S(2)}) copy-start(f32[3584,128]{0,1:T(8,128)S(1)} %collective-permute-done.3) | copy-start | bytes 5505028
  118.6 1.6 collective-permute-start.4
  120.3 8.4 %collective-permute-start.5 = (f32[256,256]{1,0:T(8,128)S(1)}, f32[256,256]{1,0:T(8,128)S(1)}, u32[]{:S(2)}, u32[]{:S(2)}) collective-permute-start(f32[256,256]{1,0:T(8,128)S(1)} %add.45), channel_id=1, source_target_pairs={{0,64},{32,96},{64,0},{96,32},{128,192},{160,224},{192,128},{224,1... | collective-permute-start | bytes 786440 | tf_op jit(solution)/shard_map/ppermute | solution.py:27
  128.8 9.5 %collective-permute-start.6 = (f32[256,256]{1,0:T(8,128)S(1)}, f32[256,256]{1,0:T(8,128)S(1)}, u32[]{:S(2)}, u32[]{:S(2)}) collective-permute-start(f32[256,256]{1,0:T(8,128)S(1)} %add.46), channel_id=1, source_target_pairs={{0,128},{32,160},{64,192},{96,224},{128,0},{160,32},{192,64},{224,... | collective-permute-start | bytes 786440 | tf_op jit(solution)/shard_map/ppermute | solution.py:27
  154.7 4.4 %copy-start.2 = (f32[3584,128]{0,1:T(8,128)S(1)}, f32[3584,128]{0,1:T(8,128)}, u32[]{:S(2)}) copy-start(f32[3584,128]{0,1:T(8,128)} %copy-done.1) | copy-start | bytes 5505028
  163.1 43.7 %collective-permute-start.7 = (f32[3584,128]{0,1:T(8,128)S(1)}, f32[3584,128]{0,1:T(8,128)S(1)}, u32[]{:S(2)}, u32[]{:S(2)}) collective-permute-start(f32[3584,128]{0,1:T(8,128)S(1)} %get-tuple-element.5), channel_id=1, source_target_pairs={{31,0},{0,1},{1,2},{2,3},{3,4},{4,5},{5,6},{6,7},{7,8},{8,9},{9,10... | collective-permute-start | bytes 5505032 | tf_op jit(solution)/shard_map/ppermute | solution.py:17
  206.8 22.6 %copy-start.4 = (f32[3584,128]{0,1:T(8,128)}, f32[3584,128]{0,1:T(8,128)S(1)}, u32[]{:S(2)}) copy-start(f32[3584,128]{0,1:T(8,128)S(1)} %collective-permute-done.7) | copy-start | bytes 5505028
  210.0 1.6 collective-permute-start.8
  211.6 8.4 %collective-permute-start.9 = (f32[256,256]{1,0:T(8,128)S(1)}, f32[256,256]{1,0:T(8,128)S(1)}, u32[]{:S(2)}, u32[]{:S(2)}) collective-permute-start(f32[256,256]{1,0:T(8,128)S(1)} %add.48), channel_id=1, source_target_pairs={{0,64},{32,96},{64,0},{96,32},{128,192},{160,224},{192,128},{224,1... | collective-permute-start | bytes 786440 | tf_op jit(solution)/shard_map/ppermute | solution.py:27
  220.1 9.3 %collective-permute-start.10 = (f32[256,256]{1,0:T(8,128)S(1)}, f32[256,256]{1,0:T(8,128)S(1)}, u32[]{:S(2)}, u32[]{:S(2)}) collective-permute-start(f32[256,256]{1,0:T(8,128)S(1)} %add.49), channel_id=1, source_target_pairs={{0,128},{32,160},{64,192},{96,224},{128,0},{160,32},{192,64},{224,... | collective-permute-start | bytes 786440 | tf_op jit(solution)/shard_map/ppermute | solution.py:27
  251.3 3.7 %collective-permute-start.11 = (f32[]{:T(128)}, f32[]{:T(128)}, u32[]{:S(2)}, u32[]{:S(2)}) collective-permute-start(f32[]{:T(128)} %get-tuple-element.3), channel_id=1, source_target_pairs={{0,1},{1,0},{2,3},{3,2},{4,5},{5,4},{6,7},{7,6},{8,9},{9,8},{10,11... | collective-permute-start | bytes 20 | tf_op jit(solution)/shard_map/ppermute | solution.py:27
  256.3 4.5 %collective-permute-start.12 = (f32[]{:T(128)}, f32[]{:T(128)}, u32[]{:S(2)}, u32[]{:S(2)}) collective-permute-start(f32[]{:T(128)} %add.51), channel_id=1, source_target_pairs={{0,2},{1,3},{2,0},{3,1},{4,6},{5,7},{6,4},{7,5},{8,10},{9,11},{10,... | collective-permute-start | bytes 20 | tf_op jit(solution)/shard_map/ppermute | solution.py:27
  261.5 7.5 %collective-permute-start.13 = (f32[]{:T(128)}, f32[]{:T(128)}, u32[]{:S(2)}, u32[]{:S(2)}) collective-permute-start(f32[]{:T(128)} %add.52), channel_id=1, source_target_pairs={{0,4},{1,5},{2,6},{3,7},{4,0},{5,1},{6,2},{7,3},{8,12},{9,13},{10,... | collective-permute-start | bytes 20 | tf_op jit(solution)/shard_map/ppermute | solution.py:27
  269.7 3.6 %collective-permute-start.14 = (f32[]{:T(128)}, f32[]{:T(128)}, u32[]{:S(2)}, u32[]{:S(2)}) collective-permute-start(f32[]{:T(128)} %add.53), channel_id=1, source_target_pairs={{0,8},{1,9},{2,10},{3,11},{4,12},{5,13},{6,14},{7,15},{8,0},{9,1},... | collective-permute-start | bytes 20 | tf_op jit(solution)/shard_map/ppermute | solution.py:27
  274.0 5.3 %collective-permute-start.15 = (f32[]{:T(128)}, f32[]{:T(128)}, u32[]{:S(2)}, u32[]{:S(2)}) collective-permute-start(f32[]{:T(128)} %add.54), channel_id=1, source_target_pairs={{0,16},{1,17},{2,18},{3,19},{4,20},{5,21},{6,22},{7,23},{8,24},{9,... | collective-permute-start | bytes 20 | tf_op jit(solution)/shard_map/ppermute | solution.py:27
